TPU v7x, 32 devices: a whole 2x2x4 slice. The times are simulated.
32 devices in a mesh: rep: 4 (over y, core), shard: 8 (over z, x).
Axes of the slice: x: 2, y: 2, z: 4, core: 2. Of those that a mesh axis runs over, the one named last changes fastest.
Arguments:
- cell_features: bfloat16 [4, 4096, 1024], P('rep', 'shard'), may hold values from -10 to 10
- upstream: bfloat16 [4, 4096, 1024], P('rep', 'shard'), may hold values from -0.119628906 to 0.119628906
- qkv_weight: bfloat16 [4, 1024, 3072], P('rep', 'shard'), may hold values from -0.1875 to 0.1875
- out_weight: bfloat16 [4, 1024, 1024], P('rep', 'shard'), may hold values from -0.1875 to 0.1875
- momentum: float32 [4, 1024, 1024], P('rep', 'shard'), may hold values from -4 to 4
- key_tiles: int32 [4, 32, 6], P('rep'), may hold values from 0 to 31, as said below
- live_blocks: int32 [4, 32], P('rep'), may hold values from 1 to 6
- step_index: int32 [], replicated, may hold values from 0 to 999
Outputs:
- layer_out: bfloat16 [4, 4096, 1024], P('rep', 'shard')
- new_weight: bfloat16 [4, 1024, 1024], P('rep', 'shard')
- new_momentum: float32 [4, 1024, 1024], P('rep', 'shard')
Inputs may be any that keep to these rules, and one draw needn't show every extreme that they name: `key_tiles`: every entry names a tile of its group. Of the 24 entries of device d's 4 query tiles (tiles d*4 to (d+1)*4 - 1), exactly 12 name tiles of device d itself (tile // 4 == d); of the others at most 2 name tiles of any one other device, and in every draw some device is named exactly 2 times.
All inputs are finite; a program needn't handle non-finite values.
Results may differ from a plain program's by a relative error of at most 0.025.
Values may be sent and summed in bfloat16 or wider, within the bound.
No kernel may reach another device: no remote copies, remote signals or barrier semaphores. Data moves between devices by JAX's collectives and lax.ppermute only.
A program may use at most 128 MiB of HBM per device.

v0:
```python
import functools
import jax
import jax.numpy as jnp
from jax import lax
from jax.sharding import PartitionSpec as P

HEADS = 16
HEAD_DIM = 64
TILE = 128
KB = 6
momentum_beta = 0.9


def shortened(value):

    def short(part):
        return part.astype(jnp.bfloat16) if part.dtype == jnp.float32 else part

    return jax.tree.map(short, value)


def partner(value, axis, bit):
    return lax.ppermute(value, axis, [(i, i ^ 1 << bit) for i in range(lax.axis_size(axis))])


def add_rows(source, shard_rows):
    return jnp.dot(source, shard_rows, preferred_element_type=jnp.float32)


def attend_tile(local_table, arrived_table, element):
    query_tile, is_remote, local_index, arrive_index, live_count = element
    model_width = query_tile.shape[1]
    from_local = local_table[local_index]
    from_remote = arrived_table[arrive_index]
    key_value = jnp.where(is_remote[:, None, None], from_remote, from_local).reshape(
        KB * TILE, 2 * model_width
    )
    query_split = query_tile.reshape(TILE, HEADS, HEAD_DIM)
    keys_split = key_value[:, :model_width].reshape(KB * TILE, HEADS, HEAD_DIM)
    values_split = key_value[:, model_width:].reshape(KB * TILE, HEADS, HEAD_DIM)
    scores = jnp.einsum(
        "qhd,khd->hqk", query_split, keys_split, preferred_element_type=jnp.float32
    ) * HEAD_DIM ** (-0.5)
    usable = jnp.arange(KB * TILE, dtype=jnp.int32) // TILE < live_count
    scores = jnp.where(usable[None, None, :], scores, jnp.float32(-1e30))
    row_max = jnp.max(scores, axis=2, keepdims=True)
    exponent = jnp.exp(scores - row_max)
    probabilities = (exponent / jnp.sum(exponent, axis=2, keepdims=True)).astype(jnp.bfloat16)
    mixture = jnp.einsum(
        "hqk,khd->qhd", probabilities, values_split, preferred_element_type=jnp.float32
    )
    return mixture.reshape(TILE, model_width).astype(jnp.bfloat16)


def swap_with(bit_number, stacked_pair):
    return jax.tree.map(
        lambda part, own: part.astype(own.dtype),
        partner(shortened(stacked_pair), "rep", bit_number),
        stacked_pair,
    )


def body(
    cell_features, upstream, qkv_weight, out_weight, momentum, key_tiles, live_blocks, step_index
):
    features = cell_features[0]
    row_count, model_width = features.shape
    tile_count = row_count // TILE
    shard_count = lax.axis_size("shard")
    my_index = lax.axis_index("shard")
    slot_count = tile_count * KB
    remote_count = slot_count - slot_count // 2
    capacity = (remote_count + shard_count - 2) // (shard_count - 1)
    requests = key_tiles[0].reshape(shard_count, slot_count)
    owners = requests // tile_count
    local_tile = requests % tile_count
    requester = jnp.arange(shard_count, dtype=jnp.int32)[:, None]
    elsewhere = owners != requester
    positions = jnp.arange(slot_count, dtype=jnp.int32)
    earlier = positions[None, :] < positions[:, None]
    same_owner = owners[:, :, None] == owners[:, None, :]
    owner_rank = jnp.sum((same_owner & earlier[None]).astype(jnp.int32), axis=2)
    owned = (owners == my_index) & elsewhere
    slot_ids = jnp.arange(capacity, dtype=jnp.int32)
    chosen = owned[:, :, None] & (owner_rank[:, :, None] == slot_ids[None, None, :])
    send_index = jnp.sum(chosen.astype(jnp.int32) * local_tile[:, :, None], axis=1).reshape(-1)
    send_valid = jnp.any(chosen, axis=1).reshape(-1)
    my_owners = lax.dynamic_index_in_dim(owners, my_index, 0, keepdims=False)
    my_ranks = lax.dynamic_index_in_dim(owner_rank, my_index, 0, keepdims=False)
    my_local = lax.dynamic_index_in_dim(local_tile, my_index, 0, keepdims=False)
    my_remote = my_owners != my_index
    arrive_index = jnp.where(my_remote, my_owners * capacity + my_ranks, 0)
    local_index = jnp.where(my_remote, 0, my_local)
    projected = add_rows(
        features, lax.all_gather(qkv_weight[0], "shard", axis=0, tiled=True)
    ).astype(jnp.bfloat16)
    picked = projected[:, model_width:].reshape(tile_count, TILE, 2 * model_width)[send_index]
    sent = jnp.where(send_valid[:, None, None], picked, jnp.zeros_like(picked)).reshape(
        shard_count, capacity, TILE, 2 * model_width
    )
    arrived = lax.all_to_all(sent, "shard", split_axis=0, concat_axis=0, tiled=True)
    arrived_table = arrived.reshape(shard_count * capacity, TILE, 2 * model_width)
    query = projected[:, :model_width].reshape(tile_count, TILE, model_width)
    local_table = projected[:, model_width:].reshape(tile_count, TILE, 2 * model_width)
    live_mine = lax.dynamic_slice_in_dim(live_blocks[0], my_index * tile_count, tile_count, 0)
    per_tile = functools.partial(attend_tile, local_table, arrived_table)
    elements = (
        query,
        my_remote.reshape(tile_count, KB),
        local_index.reshape(tile_count, KB),
        arrive_index.reshape(tile_count, KB),
        live_mine,
    )
    attended = lax.map(per_tile, elements).reshape(row_count, model_width)
    product = add_rows(attended, lax.all_gather(out_weight[0], "shard", axis=0, tiled=True))
    layer_out = (features.astype(jnp.float32) + product).astype(jnp.bfloat16)
    gradient = lax.psum_scatter(
        lax.dot_general(
            attended, upstream[0], (((0,), (0,)), ((), ())), preferred_element_type=jnp.float32
        ).astype(jnp.bfloat16),
        "shard",
        scatter_dimension=0,
        tiled=True,
    ).astype(jnp.float32)
    learn_rate = jnp.float32(50.0) / (jnp.float32(500.0) + step_index.astype(jnp.float32))
    velocity = momentum_beta * momentum[0] + gradient
    stepped = (out_weight[0].astype(jnp.float32) - learn_rate * velocity).astype(jnp.bfloat16)
    stacked_pair = jnp.stack([stepped.astype(jnp.float32), velocity])
    bit_count = lax.axis_size("rep").bit_length() - 1
    branches = [functools.partial(swap_with, bit_number) for bit_number in range(bit_count)]
    bit_choice = step_index % bit_count
    partner_pair = lax.switch(bit_choice, branches, stacked_pair)
    averaged = 0.5 * (stacked_pair + partner_pair)
    new_weight = averaged[0].astype(jnp.bfloat16)
    new_momentum = averaged[1]
    return (layer_out[None], new_weight[None], new_momentum[None])


def solution(mesh):
    placed = (
        P("rep", "shard", None),
        P("rep", "shard", None),
        P("rep", "shard", None),
        P("rep", "shard", None),
        P("rep", "shard", None),
        P("rep", None, None),
        P("rep", None),
        P(),
    )
    return jax.shard_map(
        body,
        mesh=mesh,
        in_specs=placed,
        out_specs=(P("rep", "shard", None), P("rep", "shard", None), P("rep", "shard", None)),
        check_vma=False,
    )
```

profile of v0, /device:TPU:0, one launch (start us, length us, event | category | flops | bytes accessed | tf_op | source)
XLA Modules:
  0.0 585.2 jit_solution(10328500597849223528)
XLA Ops:
  9.7 101.9 %all-gather.5.cloned.1.call-done = bf16[1,1024,3072]{2,1,0:T(8,128)(2,1)} async-done(((bf16[1,128,3072]{2,1,0:T(8,128)(2,1)}), bf16[1,1024,3072]{2,1,0:T(8,128)(2,1)}) %all-gather.5.cloned.1.call-update) | async-done | bytes 6291472 | tf_op jit(solution)/shard_map/all_gather | solution.py:95
  111.6 6.5 %fusion.21 = bf16[512,3072]{1,0:T(8,128)(2,1)S(1)} fusion(bf16[1,1024,3072]{2,1,0:T(8,128)(2,1)} %all-gather.5.cloned.1.call-done, bf16[1,512,1024]{2,1,0:T(8,128)(2,1)} %param.12), kind=kOutput, calls=%fused_computation.42 | convolution fusion | flops 3222798336 | bytes 10485760 | tf_op jit(solution)/shard_map/dot_general | solution.py:27
  120.0 4.6 gather_fusion.2
  124.7 7.2 %broadcast_select_fusion.1 = bf16[8,2,128,2048]{3,2,1,0:T(8,128)(2,1)} fusion(bf16[8,2,128,2048]{3,2,1,0:T(8,128)(2,1)} %bitcast.120, pred[8,2]{1,0:T(8,128)(4,1)S(1)} %copy.22), kind=kLoop, calls=%fused_computation.39 | loop fusion | flops 4194304 | bytes 16777232 | tf_op jit(solution)/shard_map/jit(_where)/select_n | solution.py:98
  131.9 5.1 all-to-all-start
  140.6 203.7 %all-to-all-done = bf16[8,2,128,2048]{3,2,1,0:T(8,128)(2,1)} async-done(((bf16[8,2,128,2048]{3,2,1,0:T(8,128)(2,1)}), bf16[8,2,128,2048]{3,2,1,0:T(8,128)(2,1)}, u32[]{:S(2)}, u32[]{:S(2)}) %all-to-all-start) | async-done | bytes 8388640 | tf_op jit(solution)/shard_map/all_to_all | solution.py:101
  344.3 157.9 %while.12 = (s32[]{:T(128)}, bf16[4,128,1024]{2,1,0:T(8,128)(2,1)}, pred[4,6]{1,0:T(4,128)(4,1)S(1)}, s32[4,6]{1,0:T(4,128)S(1)}, bf16[16,128,2048]{2,1,0:T(8,12...) while((s32[]{:T(128)}, bf16[4,128,1024]{2,1,0:T(8,128)(2,1)}, ...), condition=%wide.region_6.7_spmd, body=%wide.region_3.6_spmd.sunk | while | flops 413804064 | bytes 59273044 | solution.py:114
  344.3 6.0 %gather_fusion = bf16[6,128,2048]{2,1,0:T(8,128)(2,1)} fusion(bf16[16,128,2048]{2,1,0:T(8,128)(2,1)} %get-tuple-element.279, s32[1024]{0:T(1024)S(1)} %pad_clamp_fusion.5), kind=kCustom, calls=%fused_computation.clone.1 | custom fusion | bytes 6291480 | tf_op jit(solution)/shard_map/while/body/eval_jaxpr/gather | solution.py:34
  350.3 4.7 copy.33
  357.4 4.6 copy.34
  362.2 3.2 broadcast_select_fusion.5
  370.3 6.4 %fusion.70 = (f32[16,128]{1,0:T(8,128)S(1)}, f32[16,128,768]{2,1,0:T(8,128)}) fusion(pred[768]{0:T(1024)(128)(4,1)S(1)} %fusion.69, bf16[128,16,64]{0,2,1:T(8,128)(2,1)} %bitcast.121, bf16[768,16,64]{0,2,1:T(8,128)(2,1)} %bitcast.119), kind=kOutput, calls=%fused_computation.90.clone.1 | convolution fusion | flops 207618816 | bytes 8135424 | tf_op jit(solution)/shard_map/while/body/eval_jaxpr/sub | solution.py:47
  376.7 5.3 fusion.71
  383.8 6.0 %gather_fusion = bf16[6,128,2048]{2,1,0:T(8,128)(2,1)} fusion(bf16[16,128,2048]{2,1,0:T(8,128)(2,1)} %get-tuple-element.279, s32[1024]{0:T(1024)S(1)} %pad_clamp_fusion.5), kind=kCustom, calls=%fused_computation.clone.1 | custom fusion | bytes 6291480 | tf_op jit(solution)/shard_map/while/body/eval_jaxpr/gather | solution.py:34
  389.8 4.7 copy.33
  396.9 4.6 copy.34
  401.6 3.2 broadcast_select_fusion.5
  409.7 6.4 %fusion.70 = (f32[16,128]{1,0:T(8,128)S(1)}, f32[16,128,768]{2,1,0:T(8,128)}) fusion(pred[768]{0:T(1024)(128)(4,1)S(1)} %fusion.69, bf16[128,16,64]{0,2,1:T(8,128)(2,1)} %bitcast.121, bf16[768,16,64]{0,2,1:T(8,128)(2,1)} %bitcast.119), kind=kOutput, calls=%fused_computation.90.clone.1 | convolution fusion | flops 207618816 | bytes 8135424 | tf_op jit(solution)/shard_map/while/body/eval_jaxpr/sub | solution.py:47
  416.1 5.3 fusion.71
  423.3 6.0 %gather_fusion = bf16[6,128,2048]{2,1,0:T(8,128)(2,1)} fusion(bf16[16,128,2048]{2,1,0:T(8,128)(2,1)} %get-tuple-element.279, s32[1024]{0:T(1024)S(1)} %pad_clamp_fusion.5), kind=kCustom, calls=%fused_computation.clone.1 | custom fusion | bytes 6291480 | tf_op jit(solution)/shard_map/while/body/eval_jaxpr/gather | solution.py:34
  429.2 4.7 copy.33
  436.4 4.6 copy.34
  449.2 6.4 %fusion.70 = (f32[16,128]{1,0:T(8,128)S(1)}, f32[16,128,768]{2,1,0:T(8,128)}) fusion(pred[768]{0:T(1024)(128)(4,1)S(1)} %fusion.69, bf16[128,16,64]{0,2,1:T(8,128)(2,1)} %bitcast.121, bf16[768,16,64]{0,2,1:T(8,128)(2,1)} %bitcast.119), kind=kOutput, calls=%fused_computation.90.clone.1 | convolution fusion | flops 207618816 | bytes 8135424 | tf_op jit(solution)/shard_map/while/body/eval_jaxpr/sub | solution.py:47
  455.6 5.3 fusion.71
  462.8 6.0 %gather_fusion = bf16[6,128,2048]{2,1,0:T(8,128)(2,1)} fusion(bf16[16,128,2048]{2,1,0:T(8,128)(2,1)} %get-tuple-element.279, s32[1024]{0:T(1024)S(1)} %pad_clamp_fusion.5), kind=kCustom, calls=%fused_computation.clone.1 | custom fusion | bytes 6291480 | tf_op jit(solution)/shard_map/while/body/eval_jaxpr/gather | solution.py:34
  468.7 4.7 copy.33
  475.9 4.6 copy.34
  488.7 6.4 %fusion.70 = (f32[16,128]{1,0:T(8,128)S(1)}, f32[16,128,768]{2,1,0:T(8,128)}) fusion(pred[768]{0:T(1024)(128)(4,1)S(1)} %fusion.69, bf16[128,16,64]{0,2,1:T(8,128)(2,1)} %bitcast.121, bf16[768,16,64]{0,2,1:T(8,128)(2,1)} %bitcast.119), kind=kOutput, calls=%fused_computation.90.clone.1 | convolution fusion | flops 207618816 | bytes 8135424 | tf_op jit(solution)/shard_map/while/body/eval_jaxpr/sub | solution.py:47
  495.1 5.3 fusion.71
  502.2 3.9 convolution_convert_fusion
  506.9 4.2 fusion.28
  511.1 62.4 %reduce-scatter.2.cloned.1.call-done = bf16[128,1024]{1,0:T(8,128)(2,1)} async-done(((bf16[1024,1024]{1,0:T(8,128)(2,1)}), bf16[128,1024]{1,0:T(8,128)(2,1)}) %reduce-scatter.2.cloned.1.call-update) | async-done | bytes 262160 | tf_op jit(solution)/shard_map/reduce_scatter | solution.py:117
  (105 shorter events, 58.6 us)
Async XLA Ops:
  7.2 495.0 %copy-start = (bf16[1,512,1024]{2,1,0:T(8,128)(2,1)S(1)}, bf16[1,512,1024]{2,1,0:T(8,128)(2,1)}, u32[]{:S(2)}) copy-start(bf16[1,512,1024]{2,1,0:T(8,128)(2,1)} %param.13) | copy-start | bytes 3145732
  7.2 104.4 %all-gather.5.cloned.1.call-start = ((), (), s32[]{:S(2)}) async-start(), calls=%async_computation.3 | async-start | bytes 7077888 | tf_op jit(solution)/shard_map/all_gather | solution.py:95
  118.2 1.7 copy-start.1
  131.9 6.4 %copy-start.5 = (s32[1,32]{1,0:T(1,128)S(1)}, s32[1,32]{1,0:T(1,128)}, u32[]{:S(2)}) copy-start(s32[1,32]{1,0:T(1,128)} %param.18) | copy-start | bytes 388
  131.9 212.4 %all-to-all-start = ((bf16[8,2,128,2048]{3,2,1,0:T(8,128)(2,1)}), bf16[8,2,128,2048]{3,2,1,0:T(8,128)(2,1)}, u32[]{:S(2)}, u32[]{:S(2)}) async-start(bf16[8,2,128,2048]{3,2,1,0:T(8,128)(2,1)} %broadcast_select_fusion.1), calls=%async_computation | async-start | bytes 16777216 | tf_op jit(solution)/shard_map/all_to_all | solution.py:101
  136.9 370.0 %all-gather.7.cloned.1.call-start = ((), (), s32[]{:S(2)}) async-start(), calls=%async_computation.4 | async-start | bytes 2359296 | tf_op jit(solution)/shard_map/all_gather | solution.py:115
  137.7 435.9 %reduce-scatter.2.cloned.1.call-start = ((), (), s32[]{:S(2)}) async-start(), calls=%async_computation.2 | async-start | bytes 2359296 | tf_op jit(solution)/shard_map/reduce_scatter | solution.py:117
  502.2 4.7 copy-start.4
  506.9 66.7 %copy-start.2 = (bf16[1,128,1024]{2,1,0:T(8,128)(2,1)S(1)}, bf16[1,128,1024]{2,1,0:T(8,128)(2,1)}, u32[]{:S(2)}) copy-start(bf16[1,128,1024]{2,1,0:T(8,128)(2,1)} %param.15) | copy-start | bytes 786436
  506.9 66.7 %copy-start.3 = (f32[1,128,1024]{2,1,0:T(8,128)S(1)}, f32[1,128,1024]{2,1,0:T(8,128)}, u32[]{:S(2)}) copy-start(f32[1,128,1024]{2,1,0:T(8,128)} %param.16) | copy-start | bytes 1572868
  574.8 2.0 collective-permute-start
Sparse Core Ops, SparseCore 0:
  10.2 101.3 all-gather.4
  139.9 169.2 all-gather.6
  506.3 67.2 reduce-scatter.1
where the time goes:
time: 587 us; the launch traced here: 585 us
  waiting for transfers between devices  371 us (63%)
  local copies, waits for them, and re-layouts  108 us (18%)
  matrix products  61.4 us (10%)
  other arithmetic  24.6 us (4%)
  between operations  14.6 us (2%)
    all_to_all x1, waiting for transfers between devices, body(): lax.all_to_all(sent, 'shard', split_axis=0, concat_axis=0, tiled=True)  204 us
    all_gather x1, waiting for transfers between devices, body(): lax.all_gather(qkv_weight[0], 'shard', axis=0, tiled=True)  102 us
    reduce_scatter x1, waiting for transfers between devices, body(): lax.psum_scatter(lax.dot_general(attended, upstream[0], (((0,), (0,)), ((...  62.4 us
    gather x8, local copies, waits for them, and re-layouts, attend_tile(): from_remote = arrived_table[arrive_index]  42.6 us
    gather x8, local copies, waits for them, and re-layouts, attend_tile(): from_local = local_table[local_index]  28.5 us
    sub x4, matrix products, attend_tile(): exponent = jnp.exp(scores - row_max)  25.6 us
    dot_general x4, matrix products, attend_tile(): jnp.einsum('hqk,khd->qhd', probabilities, values_split, preferred_element...  21.1 us
    select_n x4, other arithmetic, attend_tile(): jnp.where(is_remote[:, None, None], from_remote, from_local)  12.7 us
  transfers between devices with their start and end apart: 5, of which 4 were waited for; matrix products, arithmetic and copies ran while one was open for 29% of the time, Pallas kernels for 0%

commit v1 on v0

--- a/solution.py
+++ b/solution.py
@@ -9,6 +9,24 @@
 TILE = 128
 KB = 6
 momentum_beta = 0.9
+
+
+def ring_gather(value, axis, dim):
+    ways, here, turn = (lax.axis_size(axis), lax.axis_index(axis), value.shape[dim])
+    dims = [n * ways if d == dim else n for d, n in enumerate(value.shape)]
+    full = lax.dynamic_update_slice_in_dim(
+        jnp.zeros(dims, value.dtype), value, here * turn, axis=dim
+    )
+    going_up = going_down = value
+    for far in range(1, ways // 2 + 1):
+        going_up = lax.ppermute(going_up, axis, [(d, (d + 1) % ways) for d in range(ways)])
+        full = lax.dynamic_update_slice_in_dim(full, going_up, (here - far) % ways * turn, axis=dim)
+        if 2 * far < ways:
+            going_down = lax.ppermute(going_down, axis, [(d, (d - 1) % ways) for d in range(ways)])
+            full = lax.dynamic_update_slice_in_dim(
+                full, going_down, (here + far) % ways * turn, axis=dim
+            )
+    return full
 
 
 def shortened(value):
@@ -91,9 +109,7 @@
     my_remote = my_owners != my_index
     arrive_index = jnp.where(my_remote, my_owners * capacity + my_ranks, 0)
     local_index = jnp.where(my_remote, 0, my_local)
-    projected = add_rows(
-        features, lax.all_gather(qkv_weight[0], "shard", axis=0, tiled=True)
-    ).astype(jnp.bfloat16)
+    projected = add_rows(features, ring_gather(qkv_weight[0], "shard", 0)).astype(jnp.bfloat16)
     picked = projected[:, model_width:].reshape(tile_count, TILE, 2 * model_width)[send_index]
     sent = jnp.where(send_valid[:, None, None], picked, jnp.zeros_like(picked)).reshape(
         shard_count, capacity, TILE, 2 * model_width

time: 587 us -> 605 us (1.031)
  starting transfers between devices: 5.45 us -> 24.5 us
    ppermute x0 -> x7, waiting for transfers between devices: none -> 105 us  [the longest x4 86.5 us: ring_gather(): lax.ppermute(going_up, axis, [(d, (d + 1) % ways) for d in range(ways)])]
    all_gather x1 -> x0, waiting for transfers between devices: 102 us -> none  [body(): lax.all_gather(qkv_weight[0], 'shard', axis=0, tiled=True)]
    ppermute x0 -> x7, starting transfers between devices: none -> 19.1 us  [the longest x4 10.4 us: ring_gather(): lax.ppermute(going_up, axis, [(d, (d + 1) % ways) for d in range(ways)])]
  transfers between devices with their start and end apart: 5 -> 11, of which waited for: 4 -> 8; matrix products, arithmetic and copies ran while one was open for 29% -> 28% of each run, Pallas kernels for 0% -> 0%
where the time goes in v1:
time: 605 us; the launch traced here: 603 us
  waiting for transfers between devices  372 us (61%)
  local copies, waits for them, and re-layouts  109 us (18%)
  matrix products  58.4 us (10%)
  other arithmetic  24.7 us (4%)
  starting transfers between devices  24.5 us (4%)
  between operations  15.1 us (2%)
    all_to_all x1, waiting for transfers between devices, body(): lax.all_to_all(sent, 'shard', split_axis=0, concat_axis=0, tiled=True)  202 us
    ppermute x4, waiting for transfers between devices, ring_gather(): lax.ppermute(going_up, axis, [(d, (d + 1) % ways) for d in range(ways)])  86.5 us
    reduce_scatter x1, waiting for transfers between devices, body(): lax.psum_scatter(lax.dot_general(attended, upstream[0], (((0,), (0,)), ((...  62.4 us
    gather x8, local copies, waits for them, and re-layouts, attend_tile(): from_remote = arrived_table[arrive_index]  42.7 us
    gather x8, local copies, waits for them, and re-layouts, attend_tile(): from_local = local_table[local_index]  28.5 us
    sub x4, matrix products, attend_tile(): exponent = jnp.exp(scores - row_max)  25.6 us
    dot_general x4, matrix products, attend_tile(): jnp.einsum('hqk,khd->qhd', probabilities, values_split, preferred_element...  21.1 us
    ppermute x3, waiting for transfers between devices, ring_gather(): lax.ppermute(going_down, axis, [(d, (d - 1) % ways) for d in range(ways)])  18.5 us
  transfers between devices with their start and end apart: 11, of which 8 were waited for; matrix products, arithmetic and copies ran while one was open for 28% of the time, Pallas kernels for 0%

profile of v1, /device:TPU:0, one launch (start us, length us, event | category | flops | bytes accessed | tf_op | source)
XLA Modules:
  0.0 603.3 jit_solution(4436289065777069354)
XLA Ops:
  15.1 29.1 %collective-permute-done.2 = bf16[128,3072]{1,0:T(8,128)(2,1)S(1)} collective-permute-done((bf16[128,3072]{1,0:T(8,128)(2,1)}, bf16[128,3072]{1,0:T(8,128)(2,1)S(1)}, u32[]{:S(2)}, u32[]{:S(2)}) %collective-permute-start.2) | collective-permute-done | bytes 786464 | tf_op jit(solution)/shard_map/ppermute | solution.py:22
  50.5 28.8 %collective-permute-done.4 = bf16[128,3072]{1,0:T(8,128)(2,1)S(1)} collective-permute-done((bf16[128,3072]{1,0:T(8,128)(2,1)S(1)}, bf16[128,3072]{1,0:T(8,128)(2,1)S(1)}, u32[]{:S(2)}, u32[]{:S(2)}) %collective-permute-start.4) | collective-permute-done | bytes 786464 | tf_op jit(solution)/shard_map/ppermute | solution.py:22
  85.2 28.6 %collective-permute-done.6 = bf16[128,3072]{1,0:T(8,128)(2,1)S(1)} collective-permute-done((bf16[128,3072]{1,0:T(8,128)(2,1)S(1)}, bf16[128,3072]{1,0:T(8,128)(2,1)S(1)}, u32[]{:S(2)}, u32[]{:S(2)}) %collective-permute-start.6) | collective-permute-done | bytes 786464 | tf_op jit(solution)/shard_map/ppermute | solution.py:22
  116.4 18.0 %collective-permute-done.7 = bf16[128,3072]{1,0:T(8,128)(2,1)S(1)} collective-permute-done((bf16[128,3072]{1,0:T(8,128)(2,1)S(1)}, bf16[128,3072]{1,0:T(8,128)(2,1)S(1)}, u32[]{:S(2)}, u32[]{:S(2)}) %collective-permute-start.7) | collective-permute-done | bytes 786464 | tf_op jit(solution)/shard_map/ppermute | solution.py:25
  140.1 4.7 gather_fusion.2
  144.8 7.2 %broadcast_select_fusion.1 = bf16[8,2,128,2048]{3,2,1,0:T(8,128)(2,1)} fusion(bf16[8,2,128,2048]{3,2,1,0:T(8,128)(2,1)} %bitcast.120, pred[8,2]{1,0:T(8,128)(4,1)S(1)} %copy.22), kind=kLoop, calls=%fused_computation.39 | loop fusion | flops 4194304 | bytes 16777232 | tf_op jit(solution)/shard_map/jit(_where)/select_n | solution.py:114
  152.0 5.1 all-to-all-start
  160.7 201.5 %all-to-all-done = bf16[8,2,128,2048]{3,2,1,0:T(8,128)(2,1)} async-done(((bf16[8,2,128,2048]{3,2,1,0:T(8,128)(2,1)}), bf16[8,2,128,2048]{3,2,1,0:T(8,128)(2,1)}, u32[]{:S(2)}, u32[]{:S(2)}) %all-to-all-start) | async-done | bytes 8388640 | tf_op jit(solution)/shard_map/all_to_all | solution.py:117
  362.2 157.8 %while.12 = (s32[]{:T(128)}, bf16[4,128,1024]{2,1,0:T(8,128)(2,1)}, pred[4,6]{1,0:T(4,128)(4,1)S(1)}, s32[4,6]{1,0:T(4,128)S(1)}, bf16[16,128,2048]{2,1,0:T(8,12...) while((s32[]{:T(128)}, bf16[4,128,1024]{2,1,0:T(8,128)(2,1)}, ...), condition=%wide.region_6.7_spmd, body=%wide.region_3.6_spmd.sunk | while | flops 413804064 | bytes 59273044 | solution.py:130
  362.2 6.0 gather_fusion
  368.2 4.7 copy.33
  375.4 4.6 copy.34
  388.2 6.4 %fusion.67 = (f32[16,128]{1,0:T(8,128)S(1)}, f32[16,128,768]{2,1,0:T(8,128)}) fusion(pred[768]{0:T(1024)(128)(4,1)S(1)} %fusion.66, bf16[128,16,64]{0,2,1:T(8,128)(2,1)} %bitcast.121, bf16[768,16,64]{0,2,1:T(8,128)(2,1)} %bitcast.119), kind=kOutput, calls=%fused_computation.97.clone.1 | convolution fusion | flops 207618816 | bytes 8135424 | tf_op jit(solution)/shard_map/while/body/eval_jaxpr/sub | solution.py:65
  394.6 5.3 fusion.68
  401.7 6.0 gather_fusion
  407.7 4.7 copy.33
  414.8 4.6 copy.34
  427.6 6.4 %fusion.67 = (f32[16,128]{1,0:T(8,128)S(1)}, f32[16,128,768]{2,1,0:T(8,128)}) fusion(pred[768]{0:T(1024)(128)(4,1)S(1)} %fusion.66, bf16[128,16,64]{0,2,1:T(8,128)(2,1)} %bitcast.121, bf16[768,16,64]{0,2,1:T(8,128)(2,1)} %bitcast.119), kind=kOutput, calls=%fused_computation.97.clone.1 | convolution fusion | flops 207618816 | bytes 8135424 | tf_op jit(solution)/shard_map/while/body/eval_jaxpr/sub | solution.py:65
  434.0 5.3 fusion.68
  441.1 6.0 gather_fusion
  447.1 4.7 copy.33
  454.3 4.6 copy.34
  467.1 6.4 %fusion.67 = (f32[16,128]{1,0:T(8,128)S(1)}, f32[16,128,768]{2,1,0:T(8,128)}) fusion(pred[768]{0:T(1024)(128)(4,1)S(1)} %fusion.66, bf16[128,16,64]{0,2,1:T(8,128)(2,1)} %bitcast.121, bf16[768,16,64]{0,2,1:T(8,128)(2,1)} %bitcast.119), kind=kOutput, calls=%fused_computation.97.clone.1 | convolution fusion | flops 207618816 | bytes 8135424 | tf_op jit(solution)/shard_map/while/body/eval_jaxpr/sub | solution.py:65
  473.5 5.3 fusion.68
  480.6 6.0 gather_fusion
  486.5 4.7 copy.33
  493.7 4.6 copy.34
  506.5 6.4 %fusion.67 = (f32[16,128]{1,0:T(8,128)S(1)}, f32[16,128,768]{2,1,0:T(8,128)}) fusion(pred[768]{0:T(1024)(128)(4,1)S(1)} %fusion.66, bf16[128,16,64]{0,2,1:T(8,128)(2,1)} %bitcast.121, bf16[768,16,64]{0,2,1:T(8,128)(2,1)} %bitcast.119), kind=kOutput, calls=%fused_computation.97.clone.1 | convolution fusion | flops 207618816 | bytes 8135424 | tf_op jit(solution)/shard_map/while/body/eval_jaxpr/sub | solution.py:65
  512.9 5.3 fusion.68
  520.0 4.0 convolution_convert_fusion.1
  524.8 4.1 fusion.24
  529.0 62.4 %reduce-scatter.2.cloned.1.call-done = bf16[128,1024]{1,0:T(8,128)(2,1)} async-done(((bf16[1024,1024]{1,0:T(8,128)(2,1)}), bf16[128,1024]{1,0:T(8,128)(2,1)}) %reduce-scatter.2.cloned.1.call-update) | async-done | bytes 262160 | tf_op jit(solution)/shard_map/reduce_scatter | solution.py:133
  (129 shorter events, 88.7 us)
Async XLA Ops:
  7.2 512.8 %copy-start = (bf16[1,512,1024]{2,1,0:T(8,128)(2,1)S(1)}, bf16[1,512,1024]{2,1,0:T(8,128)(2,1)}, u32[]{:S(2)}) copy-start(bf16[1,512,1024]{2,1,0:T(8,128)(2,1)} %param.13) | copy-start | bytes 3145732
  7.2 40.2 %copy-start.3 = (bf16[1,128,3072]{2,1,0:T(8,128)(2,1)S(1)}, bf16[1,128,3072]{2,1,0:T(8,128)(2,1)}, u32[]{:S(2)}) copy-start(bf16[1,128,3072]{2,1,0:T(8,128)(2,1)} %param.14) | copy-start | bytes 2359300
  7.2 37.0 %collective-permute-start.2 = (bf16[128,3072]{1,0:T(8,128)(2,1)}, bf16[128,3072]{1,0:T(8,128)(2,1)S(1)}, u32[]{:S(2)}, u32[]{:S(2)}) collective-permute-start(bf16[128,3072]{1,0:T(8,128)(2,1)} %bitcast.124), channel_id=1, source_target_pairs={{0,1},{1,2},{2,3},{3,4},{4,5},{5,6},{6,7},{7,0},{8,9},{9,10},{10,1... | collective-permute-start | bytes 2359304 | tf_op jit(solution)/shard_map/ppermute | solution.py:22
  10.2 37.2 %collective-permute-start.3 = (bf16[128,3072]{1,0:T(8,128)(2,1)}, bf16[128,3072]{1,0:T(8,128)(2,1)S(1)}, u32[]{:S(2)}, u32[]{:S(2)}) collective-permute-start(bf16[128,3072]{1,0:T(8,128)(2,1)} %bitcast.125), channel_id=1, source_target_pairs={{0,7},{1,0},{2,1},{3,2},{4,3},{5,4},{6,5},{7,6},{8,15},{9,8},{10,9... | collective-permute-start | bytes 2359304 | tf_op jit(solution)/shard_map/ppermute | solution.py:25
  44.2 35.2 %collective-permute-start.4 = (bf16[128,3072]{1,0:T(8,128)(2,1)S(1)}, bf16[128,3072]{1,0:T(8,128)(2,1)S(1)}, u32[]{:S(2)}, u32[]{:S(2)}) collective-permute-start(bf16[128,3072]{1,0:T(8,128)(2,1)S(1)} %collective-permute-done.2), channel_id=1, source_target_pairs={{0,1},{1,2},{2,3},{3,4},{4,5},{5,6},{6,7},{7,0},{8,9},{9,10},{10,1... | collective-permute-start | bytes 2359304 | tf_op jit(solution)/shard_map/ppermute | solution.py:22
  47.3 87.2 %copy-start.5 = (bf16[1,512,1024]{2,1,0:T(8,128)(2,1)S(1)}, bf16[1,512,1024]{2,1,0:T(8,128)(2,1)}, u32[]{:S(2)}) copy-start(bf16[1,512,1024]{2,1,0:T(8,128)(2,1)} %param.12) | copy-start | bytes 3145732
  47.4 35.1 %collective-permute-start.5 = (bf16[128,3072]{1,0:T(8,128)(2,1)S(1)}, bf16[128,3072]{1,0:T(8,128)(2,1)S(1)}, u32[]{:S(2)}, u32[]{:S(2)}) collective-permute-start(bf16[128,3072]{1,0:T(8,128)(2,1)S(1)} %collective-permute-done.3), channel_id=1, source_target_pairs={{0,7},{1,0},{2,1},{3,2},{4,3},{5,4},{6,5},{7,6},{8,15},{9,8},{10,9... | collective-permute-start | bytes 2359304 | tf_op jit(solution)/shard_map/ppermute | solution.py:25
  79.4 34.4 %collective-permute-start.6 = (bf16[128,3072]{1,0:T(8,128)(2,1)S(1)}, bf16[128,3072]{1,0:T(8,128)(2,1)S(1)}, u32[]{:S(2)}, u32[]{:S(2)}) collective-permute-start(bf16[128,3072]{1,0:T(8,128)(2,1)S(1)} %collective-permute-done.4), channel_id=1, source_target_pairs={{0,1},{1,2},{2,3},{3,4},{4,5},{5,6},{6,7},{7,0},{8,9},{9,10},{10,1... | collective-permute-start | bytes 2359304 | tf_op jit(solution)/shard_map/ppermute | solution.py:22
  82.5 51.9 %collective-permute-start.7 = (bf16[128,3072]{1,0:T(8,128)(2,1)S(1)}, bf16[128,3072]{1,0:T(8,128)(2,1)S(1)}, u32[]{:S(2)}, u32[]{:S(2)}) collective-permute-start(bf16[128,3072]{1,0:T(8,128)(2,1)S(1)} %collective-permute-done.5), channel_id=1, source_target_pairs={{0,7},{1,0},{2,1},{3,2},{4,3},{5,4},{6,5},{7,6},{8,15},{9,8},{10,9... | collective-permute-start | bytes 2359304 | tf_op jit(solution)/shard_map/ppermute | solution.py:25
  113.8 20.7 %collective-permute-start.8 = (bf16[128,3072]{1,0:T(8,128)(2,1)S(1)}, bf16[128,3072]{1,0:T(8,128)(2,1)S(1)}, u32[]{:S(2)}, u32[]{:S(2)}) collective-permute-start(bf16[128,3072]{1,0:T(8,128)(2,1)S(1)} %collective-permute-done.6), channel_id=1, source_target_pairs={{0,1},{1,2},{2,3},{3,4},{4,5},{5,6},{6,7},{7,0},{8,9},{9,10},{10,1... | collective-permute-start | bytes 2359304 | tf_op jit(solution)/shard_map/ppermute | solution.py:22
  138.2 1.6 copy-start.1
  152.0 6.4 %copy-start.7 = (s32[1,32]{1,0:T(1,128)S(1)}, s32[1,32]{1,0:T(1,128)}, u32[]{:S(2)}) copy-start(s32[1,32]{1,0:T(1,128)} %param.18) | copy-start | bytes 388
  152.0 210.3 %all-to-all-start = ((bf16[8,2,128,2048]{3,2,1,0:T(8,128)(2,1)}), bf16[8,2,128,2048]{3,2,1,0:T(8,128)(2,1)}, u32[]{:S(2)}, u32[]{:S(2)}) async-start(bf16[8,2,128,2048]{3,2,1,0:T(8,128)(2,1)} %broadcast_select_fusion.1), calls=%async_computation | async-start | bytes 16777216 | tf_op jit(solution)/shard_map/all_to_all | solution.py:117
  157.0 367.8 %all-gather.3.cloned.1.call-start = ((), (), s32[]{:S(2)}) async-start(), calls=%async_computation.3 | async-start | bytes 2359296 | tf_op jit(solution)/shard_map/all_gather | solution.py:131
  157.8 433.6 %reduce-scatter.2.cloned.1.call-start = ((), (), s32[]{:S(2)}) async-start(), calls=%async_computation.2 | async-start | bytes 2359296 | tf_op jit(solution)/shard_map/reduce_scatter | solution.py:133
  520.0 4.8 copy-start.6
  524.0 67.4 %copy-start.2 = (bf16[1,128,1024]{2,1,0:T(8,128)(2,1)S(1)}, bf16[1,128,1024]{2,1,0:T(8,128)(2,1)}, u32[]{:S(2)}) copy-start(bf16[1,128,1024]{2,1,0:T(8,128)(2,1)} %param.15) | copy-start | bytes 786436
  524.0 67.4 %copy-start.4 = (f32[1,128,1024]{2,1,0:T(8,128)S(1)}, f32[1,128,1024]{2,1,0:T(8,128)}, u32[]{:S(2)}) copy-start(f32[1,128,1024]{2,1,0:T(8,128)} %param.16) | copy-start | bytes 1572868
  592.6 2.0 collective-permute-start
Sparse Core Ops, SparseCore 0:
  160.0 167.0 all-gather.2
  524.1 67.2 reduce-scatter.1
